TPU v7x, 512 devices: a whole 4x8x8 slice. The times are simulated.
512 devices in a mesh: col: 8 (over z), tile: 64 (over y, x, core).
Axes of the slice: x: 4, y: 8, z: 8, core: 2. Of those that a mesh axis runs over, the one named last changes fastest.
Arguments:
- panel_factor: bfloat16 [8, 64, 2, 512, 512], P('col', 'tile'), may hold values from -0.15625 to 0.15625
- panel_cotangent: bfloat16 [8, 64, 2, 512, 512], P('col', 'tile'), may hold values from -1.5 to 1.5
- diag_factor: bfloat16 [8, 512, 512], P('col'), as said below
- diag_inverse: bfloat16 [8, 512, 512], P('col'), as said below
- diag_cotangent: float32 [8, 512, 512], P('col', 'tile'), may hold values from -6 to 6
- tile_count: int32 [8, 64], P('col', 'tile'), may hold values from 1 to 2, as said below
- tile_rows: int32 [8, 64, 2], P('col', 'tile'), may hold values from 1 to 255, as said below
Outputs:
- panel_adjoint: bfloat16 [8, 64, 2, 512, 512], P('col', 'tile')
- diag_adjoint: float32 [8, 512, 512], P('col', 'tile')
Inputs may be any that keep to these rules, and one draw needn't show every extreme that they name: `tile_count`: every device holds 1 to 2 live tiles of each panel column, in its first slots; in every column some device holds 2. `tile_rows`: in column c the live slots name distinct block rows; exactly one live slot names row c + 1, every other slot names a row of c + 2 or more. `diag_factor`: lower triangular with diagonal entries between 0.8 and 1.6. `diag_inverse`: lower triangular with diagonal entries between 0.8 and 1.6.
All inputs are finite; a program needn't handle non-finite values.
Results may differ from a plain program's by a relative error of at most 0.0044.
Values sent between devices are 32-bit elements; how exact they have to be, the bound alone decides.
No kernel may reach another device: no remote copies, remote signals or barrier semaphores. Data moves between devices by JAX's collectives and lax.ppermute only.
A program may use at most 128 MiB of HBM per device.

v0:
```python
import jax
import jax.numpy as jnp
from jax import lax
from jax.sharding import PartitionSpec as P


def passed_along(value, axis, by):
    count = lax.axis_size(axis)
    pairs = [(i, i + by) for i in range(count) if 0 <= i + by < count]
    return lax.ppermute(value, axis, pairs)


def symmetrize(matrix):
    strict = jnp.tril(matrix, -1)
    return strict + strict.T + jnp.diag(jnp.diagonal(matrix))


def on_device(
    panel_factor, panel_cotangent, diag_factor, diag_inverse, diag_cotangent, tile_count, tile_rows
):
    full = lax.Precision.HIGHEST
    factors = panel_factor[0, 0]
    cotangent = panel_cotangent[0, 0]
    lower = diag_factor[0]
    inverse = diag_inverse[0]
    width = lower.shape[0]
    rows_dev = diag_cotangent.shape[1]
    slot_count = factors.shape[0]
    column = lax.axis_index("col")
    groups = lax.axis_size("col")
    row_start = lax.axis_index("tile") * rows_dev
    live_slot = jnp.arange(slot_count) < tile_count[0, 0]
    link_flag = live_slot & (tile_rows[0, 0] == column + 1)
    solved = jnp.einsum("sij,jk->sik", cotangent, inverse, preferred_element_type=jnp.float32)
    rounded = jnp.where(
        live_slot[:, None, None], solved.astype(jnp.bfloat16), jnp.zeros_like(cotangent)
    )
    panel_terms = -jnp.einsum("sij,sik->jk", rounded, factors, preferred_element_type=jnp.float32)
    own_rows = lax.dynamic_slice_in_dim(panel_terms, row_start, rows_dev, 0) + diag_cotangent[0]
    panel_terms = lax.dynamic_update_slice_in_dim(panel_terms, own_rows, row_start, 0)
    chosen = jnp.sum(jnp.where(link_flag[:, None, None], factors, jnp.zeros_like(factors)), axis=0)
    link_part = jnp.dot(chosen, inverse, preferred_element_type=jnp.float32)
    summed, link_wide = lax.psum((panel_terms, link_part), "tile")
    inverse_wide = inverse.astype(jnp.float32)
    curvature = jnp.dot(lower.astype(jnp.float32).T, summed, precision=full)
    symmetric = symmetrize(curvature)
    own_map = 0.5 * jnp.dot(
        inverse_wide.T, jnp.dot(symmetric, inverse_wide, precision=full), precision=full
    )
    own_cols = lax.dynamic_slice_in_dim(own_map, row_start, rows_dev, 1)
    link_cols = lax.dynamic_slice_in_dim(link_wide, row_start, rows_dev, 1)
    incoming = jnp.zeros((width, width), jnp.float32)
    for sweep in range(groups - 1):
        advanced = own_cols + jnp.dot(
            link_wide.T, jnp.dot(incoming, link_cols, precision=full), precision=full
        )
        arrived = passed_along(advanced, "col", -1)
        incoming = lax.all_gather(arrived, "tile", axis=1, tiled=True)
    product = jnp.dot(incoming, link_wide, precision=full)
    link_rows = lax.dynamic_slice_in_dim(link_wide, row_start, rows_dev, 1)
    own_part = lax.dynamic_slice_in_dim(own_map, row_start, rows_dev, 0)
    diag_rows = own_part + jnp.dot(link_rows.T, product, precision=full)
    adjusted = (solved - 2.0 * product[None]).astype(jnp.bfloat16)
    panel_out = jnp.where(link_flag[:, None, None], adjusted, rounded)
    return (panel_out[None, None], diag_rows[None])


def solution(mesh):
    in_specs = (
        P("col", "tile", None, None, None),
        P("col", "tile", None, None, None),
        P("col", None, None),
        P("col", None, None),
        P("col", "tile", None),
        P("col", "tile"),
        P("col", "tile", None),
    )
    out_specs = (P("col", "tile", None, None, None), P("col", "tile", None))
    return jax.shard_map(
        on_device, mesh=mesh, in_specs=in_specs, out_specs=out_specs, check_vma=False
    )
```

profile of v0, /device:TPU:1, one launch (start us, length us, event | category | flops | bytes accessed | tf_op | source)
XLA Modules:
  0.0 887.5 jit_solution(10775126027155299674)
XLA Ops:
  8.7 1.6 fusion.5
  10.3 2.5 fusion.20
  12.7 2.1 fusion.6
  14.8 2.7 fusion
  18.6 204.7 %all-reduce.3.cloned.1.call-done = (f32[512,512]{1,0:T(8,128)}, f32[512,512]{1,0:T(8,128)}) async-done(((f32[512,512]{1,0:T(8,128)}, f32[512,512]{1,0:T(8,128)}), (f32[512,512]{1,0:T(8,128)}, f32[512,512]{1,0:T(8,128)})) %all-reduce.3.cloned.1.call-update) | async-done | bytes 2097168 | tf_op jit(solution)/shard_map/psum | solution.py:43
  224.5 3.2 fusion.15
  227.7 1.6 copy.14
  229.3 4.5 gather_fusion
  233.8 2.5 fusion.8
  239.5 3.2 collective-permute-done
  243.3 84.6 %all-gather.8.cloned.1.call-done = f32[512,512]{0,1:T(8,128)} async-done(((f32[512,8]{0,1:T(8,128)}), f32[512,512]{0,1:T(8,128)}) %all-gather.8.cloned.1.call-update) | async-done | bytes 1048592 | tf_op jit(solution)/shard_map/all_gather | solution.py:58
  327.9 3.1 fusion.38
  333.1 3.2 collective-permute-done.1
  336.9 81.4 %all-gather.10.cloned.1.call-done = f32[512,512]{0,1:T(8,128)} async-done(((f32[512,8]{0,1:T(8,128)}), f32[512,512]{0,1:T(8,128)}) %all-gather.10.cloned.1.call-update) | async-done | bytes 1048592 | tf_op jit(solution)/shard_map/all_gather | solution.py:58
  418.3 3.1 fusion.36
  423.4 3.2 collective-permute-done.2
  427.5 81.2 %all-gather.12.cloned.1.call-done = f32[512,512]{0,1:T(8,128)} async-done(((f32[512,8]{0,1:T(8,128)}), f32[512,512]{0,1:T(8,128)}) %all-gather.12.cloned.1.call-update) | async-done | bytes 1048592 | tf_op jit(solution)/shard_map/all_gather | solution.py:58
  508.6 3.1 fusion.34
  513.8 3.2 collective-permute-done.3
  517.6 81.4 %all-gather.14.cloned.1.call-done = f32[512,512]{0,1:T(8,128)} async-done(((f32[512,8]{0,1:T(8,128)}), f32[512,512]{0,1:T(8,128)}) %all-gather.14.cloned.1.call-update) | async-done | bytes 1048592 | tf_op jit(solution)/shard_map/all_gather | solution.py:58
  599.0 3.1 fusion.32
  604.1 3.2 collective-permute-done.4
  608.0 81.4 %all-gather.16.cloned.1.call-done = f32[512,512]{0,1:T(8,128)} async-done(((f32[512,8]{0,1:T(8,128)}), f32[512,512]{0,1:T(8,128)}) %all-gather.16.cloned.1.call-update) | async-done | bytes 1048592 | tf_op jit(solution)/shard_map/all_gather | solution.py:58
  689.3 3.1 fusion.30
  694.5 3.2 collective-permute-done.5
  698.3 81.4 %all-gather.18.cloned.1.call-done = f32[512,512]{0,1:T(8,128)} async-done(((f32[512,8]{0,1:T(8,128)}), f32[512,512]{0,1:T(8,128)}) %all-gather.18.cloned.1.call-update) | async-done | bytes 1048592 | tf_op jit(solution)/shard_map/all_gather | solution.py:58
  779.7 3.1 fusion.28
  785.0 3.0 collective-permute-done.6
  788.6 81.4 %all-gather.20.cloned.1.call-done = f32[512,512]{0,1:T(8,128)} async-done(((f32[512,8]{0,1:T(8,128)}), f32[512,512]{0,1:T(8,128)}) %all-gather.20.cloned.1.call-update) | async-done | bytes 1048592 | tf_op jit(solution)/shard_map/all_gather | solution.py:58
  870.0 3.1 broadcast_multiply_fusion
  873.1 2.9 fusion.1
  876.7 3.9 fusion.3
  (67 shorter events, 23.8 us)
Async XLA Ops:
  7.2 5.5 copy-start
  7.2 5.5 copy-start.2
  7.2 216.2 %all-reduce.3.cloned.1.call-start = ((), (), s32[]{:S(2)}) async-start(), calls=%async_computation.7 | async-start | bytes 4194304 | tf_op jit(solution)/shard_map/psum | solution.py:43
  14.8 2.7 copy-start.7
  17.5 207.0 %copy-start.6 = (bf16[1,512,512]{2,1,0:T(8,128)(2,1)S(1)}, bf16[1,512,512]{2,1,0:T(8,128)(2,1)}, u32[]{:S(2)}) copy-start(bf16[1,512,512]{2,1,0:T(8,128)(2,1)} %param.9) | copy-start | bytes 1572868
  17.5 1.0 copy-start.5
  18.5 309.4 %all-gather.8.cloned.1.call-start = ((), (), s32[]{:S(2)}) async-start(), calls=%async_computation | async-start | bytes 1064960 | tf_op jit(solution)/shard_map/all_gather | solution.py:58
  233.8 2.5 copy-start.3
  236.3 1.2 copy-start.1
  237.5 545.3 %copy-start.4 = (f32[512,512]{1,0:T(8,128)}, f32[512,512]{1,0:T(8,128)S(1)}, u32[]{:S(2)}) copy-start(f32[512,512]{1,0:T(8,128)S(1)} %convolution_multiply_fusion) | copy-start | bytes 3145732
  238.2 4.5 collective-permute-start
  242.7 0.6 copy-start.8
  243.3 175.0 %all-gather.10.cloned.1.call-start = ((), (), s32[]{:S(2)}) async-start(), calls=%async_computation.1 | async-start | bytes 1064960 | tf_op jit(solution)/shard_map/all_gather | solution.py:58
  331.8 4.5 collective-permute-start.1
  336.2 0.6 copy-start.9
  336.9 171.8 %all-gather.12.cloned.1.call-start = ((), (), s32[]{:S(2)}) async-start(), calls=%async_computation.2 | async-start | bytes 1064960 | tf_op jit(solution)/shard_map/all_gather | solution.py:58
  422.1 4.5 collective-permute-start.2
  426.6 0.6 copy-start.10
  427.2 171.8 %all-gather.14.cloned.1.call-start = ((), (), s32[]{:S(2)}) async-start(), calls=%async_computation.3 | async-start | bytes 1064960 | tf_op jit(solution)/shard_map/all_gather | solution.py:58
  512.5 4.5 collective-permute-start.3
  516.9 0.6 copy-start.11
  517.6 171.8 %all-gather.16.cloned.1.call-start = ((), (), s32[]{:S(2)}) async-start(), calls=%async_computation.4 | async-start | bytes 1064960 | tf_op jit(solution)/shard_map/all_gather | solution.py:58
  602.8 4.5 collective-permute-start.4
  607.3 0.6 copy-start.12
  607.9 171.8 %all-gather.18.cloned.1.call-start = ((), (), s32[]{:S(2)}) async-start(), calls=%async_computation.5 | async-start | bytes 1064960 | tf_op jit(solution)/shard_map/all_gather | solution.py:58
  693.2 4.5 collective-permute-start.5
  697.6 0.6 copy-start.13
  698.3 171.8 %all-gather.20.cloned.1.call-start = ((), (), s32[]{:S(2)}) async-start(), calls=%async_computation.6 | async-start | bytes 1064960 | tf_op jit(solution)/shard_map/all_gather | solution.py:58
  783.5 4.5 collective-permute-start.6
  788.0 0.6 copy-start.14
Sparse Core Ops, SparseCore 0:
  18.7 204.6 all-reduce.2
  243.4 84.4 all-gather.7
  337.0 81.2 all-gather.9
  427.3 81.2 all-gather.11
  517.7 81.2 all-gather.13
  608.0 81.2 all-gather.15
  698.4 81.2 all-gather.17
  788.8 81.2 all-gather.19
where the time goes:
time: 888 us; the launch traced here: 887 us
  waiting for transfers between devices  799 us (90%)
  matrix products  43.5 us (5%)
  between operations  15.2 us (2%)
  local copies, waits for them, and re-layouts  12.2 us (1%)
  starting transfers between devices  9.75 us (1%)
    all_gather x7, waiting for transfers between devices, on_device(): incoming = lax.all_gather(arrived, 'tile', axis=1, tiled=True)  573 us
    psum x1, waiting for transfers between devices, on_device(): summed, link_wide = lax.psum((panel_terms, link_part), 'tile')  205 us
    ppermute x7, waiting for transfers between devices, passed_along(): return lax.ppermute(value, axis, pairs)  22.1 us
    dot_general x6, matrix products, on_device(): jnp.dot(incoming, link_cols, precision=full)  18.8 us
  transfers between devices with their start and end apart: 15, of which 15 were waited for; matrix products, arithmetic and copies ran while one was open for 0% of the time, Pallas kernels for 0%

commit v1 on v0

--- a/solution.py
+++ b/solution.py
@@ -55,7 +55,16 @@
             link_wide.T, jnp.dot(incoming, link_cols, precision=full), precision=full
         )
         arrived = passed_along(advanced, "col", -1)
-        incoming = lax.all_gather(arrived, "tile", axis=1, tiled=True)
+
+        def write_steps_all(target, group_axis, along_dim):
+            store = []
+            for _ in range(lax.axis_size(group_axis)):
+                store.append(target)
+            return jnp.concatenate(
+                lax.all_to_all(jnp.stack(store), group_axis, 0, 0), axis=along_dim
+            )
+
+        incoming = write_steps_all(arrived, "tile", along_dim=1)
     product = jnp.dot(incoming, link_wide, precision=full)
     link_rows = lax.dynamic_slice_in_dim(link_wide, row_start, rows_dev, 1)
     own_part = lax.dynamic_slice_in_dim(own_map, row_start, rows_dev, 0)

time: 888 us -> 565 us (0.64)
  waiting for transfers between devices: 799 us -> 232 us
  blocking collectives: 0 us -> 250 us
    all_gather x7 -> x0, waiting for transfers between devices: 573 us -> none  [on_device(): incoming = lax.all_gather(arrived, 'tile', axis=1, tiled=True)]
    all_to_all x0 -> x7, blocking collectives: none -> 250 us  [write_steps_all(): lax.all_to_all(jnp.stack(store), group_axis, 0, 0)]
  transfers between devices with their start and end apart: 15 -> 8, of which waited for: 15 -> 8; matrix products, arithmetic and copies ran while one was open for 0% -> 0% of each run, Pallas kernels for 0% -> 0%
where the time goes in v1:
time: 565 us; the launch traced here: 562 us
  blocking collectives  250 us (44%)
  waiting for transfers between devices  232 us (41%)
  matrix products  40.2 us (7%)
  between operations  15 us (3%)
  starting transfers between devices  9.06 us (2%)
  local copies, waits for them, and re-layouts  7.83 us (1%)
  other arithmetic  7.52 us (1%)
    all_to_all x7, blocking collectives, write_steps_all(): lax.all_to_all(jnp.stack(store), group_axis, 0, 0)  250 us
    psum x1, waiting for transfers between devices, on_device(): summed, link_wide = lax.psum((panel_terms, link_part), 'tile')  205 us
    ppermute x7, waiting for transfers between devices, passed_along(): return lax.ppermute(value, axis, pairs)  27.1 us
    dot_general x6, matrix products, on_device(): jnp.dot(incoming, link_cols, precision=full)  11.5 us
  transfers between devices with their start and end apart: 8, of which 8 were waited for; matrix products, arithmetic and copies ran while one was open for 0% of the time, Pallas kernels for 0%

profile of v1, /device:TPU:1, one launch (start us, length us, event | category | flops | bytes accessed | tf_op | source)
XLA Modules:
  0.0 561.9 jit_solution(5562442708454797229)
XLA Ops:
  8.7 1.6 fusion.19
  10.3 2.5 fusion.34
  13.5 3.8 fusion
  18.6 204.7 %all-reduce.3.cloned.1.call-done = (f32[512,512]{1,0:T(8,128)}, f32[512,512]{1,0:T(8,128)}) async-done(((f32[512,512]{1,0:T(8,128)}, f32[512,512]{1,0:T(8,128)}), (f32[512,512]{1,0:T(8,128)}, f32[512,512]{1,0:T(8,128)})) %all-reduce.3.cloned.1.call-update) | async-done | bytes 2097168 | tf_op jit(solution)/shard_map/psum | solution.py:43
  224.4 3.3 fusion.29
  227.7 1.6 copy.21
  229.3 4.5 gather_fusion
  233.9 2.4 fusion.22
  239.5 3.2 collective-permute-done
  242.8 39.2 %all_to_all.35 = f32[64,512,8]{1,2,0:T(8,128)S(1)} all-to-all(f32[64,512,8]{1,2,0:T(8,128)S(1)} %stack.14), channel_id=1, replica_groups=mesh['col'=8,'tile'=64] {'tile'}, dimensions={0} | all-to-all | bytes 2097152 | tf_op jit(solution)/shard_map/all_to_all | solution.py:64
  282.0 1.9 fusion.16
  286.6 3.2 collective-permute-done.1
  289.9 35.4 %all_to_all.36 = f32[64,512,8]{1,2,0:T(8,128)S(1)} all-to-all(f32[64,512,8]{1,2,0:T(8,128)S(1)} %stack.15), channel_id=1, replica_groups=mesh['col'=8,'tile'=64] {'tile'}, dimensions={0} | all-to-all | bytes 2097152 | tf_op jit(solution)/shard_map/all_to_all | solution.py:64
  325.3 1.9 fusion.14
  329.9 3.2 collective-permute-done.2
  333.2 35.4 %all_to_all.37 = f32[64,512,8]{1,2,0:T(8,128)S(1)} all-to-all(f32[64,512,8]{1,2,0:T(8,128)S(1)} %stack.16), channel_id=1, replica_groups=mesh['col'=8,'tile'=64] {'tile'}, dimensions={0} | all-to-all | bytes 2097152 | tf_op jit(solution)/shard_map/all_to_all | solution.py:64
  368.6 1.9 fusion.12
  370.5 1.4 convolution_add_fusion.4
  373.3 3.6 collective-permute-done.3
  377.0 35.1 %all_to_all.38 = f32[64,512,8]{1,2,0:T(8,128)S(1)} all-to-all(f32[64,512,8]{1,2,0:T(8,128)S(1)} %stack.17), channel_id=1, replica_groups=mesh['col'=8,'tile'=64] {'tile'}, dimensions={0} | all-to-all | bytes 2097152 | tf_op jit(solution)/shard_map/all_to_all | solution.py:64
  412.1 1.9 fusion.10
  416.7 4.7 collective-permute-done.4
  421.5 35.1 %all_to_all.39 = f32[64,512,8]{1,2,0:T(8,128)S(1)} all-to-all(f32[64,512,8]{1,2,0:T(8,128)S(1)} %stack.18), channel_id=1, replica_groups=mesh['col'=8,'tile'=64] {'tile'}, dimensions={0} | all-to-all | bytes 2097152 | tf_op jit(solution)/shard_map/all_to_all | solution.py:64
  456.6 1.9 fusion.8
  461.3 4.7 collective-permute-done.5
  466.1 35.1 %all_to_all.40 = f32[64,512,8]{1,2,0:T(8,128)S(1)} all-to-all(f32[64,512,8]{1,2,0:T(8,128)S(1)} %stack.19), channel_id=1, replica_groups=mesh['col'=8,'tile'=64] {'tile'}, dimensions={0} | all-to-all | bytes 2097152 | tf_op jit(solution)/shard_map/all_to_all | solution.py:64
  501.2 1.9 fusion.6
  505.9 4.7 collective-permute-done.6
  510.6 35.1 %all_to_all.41 = f32[64,512,8]{1,2,0:T(8,128)S(1)} all-to-all(f32[64,512,8]{1,2,0:T(8,128)S(1)} %stack.20), channel_id=1, replica_groups=mesh['col'=8,'tile'=64] {'tile'}, dimensions={0} | all-to-all | bytes 2097152 | tf_op jit(solution)/shard_map/all_to_all | solution.py:64
  545.8 2.8 broadcast_multiply_fusion
  548.6 3.0 fusion.1
  552.3 2.8 fusion.3
  (48 shorter events, 23.5 us)
Async XLA Ops:
  7.2 5.6 copy-start
  7.2 216.1 %all-reduce.3.cloned.1.call-start = ((), (), s32[]{:S(2)}) async-start(), calls=%async_computation.7 | async-start | bytes 4194304 | tf_op jit(solution)/shard_map/psum | solution.py:43
  8.0 4.8 copy-start.4
  13.4 3.8 copy-start.2
  13.5 3.8 copy-start.8
  18.6 205.9 %copy-start.7 = (bf16[1,512,512]{2,1,0:T(8,128)(2,1)S(1)}, bf16[1,512,512]{2,1,0:T(8,128)(2,1)}, u32[]{:S(2)}) copy-start(bf16[1,512,512]{2,1,0:T(8,128)(2,1)} %param.9) | copy-start | bytes 1572868
  227.7 6.2 %copy-start.5 = (bf16[1,512,512]{2,1,0:T(8,128)(2,1)S(1)}, bf16[1,512,512]{2,1,0:T(8,128)(2,1)}, u32[]{:S(2)}) copy-start(bf16[1,512,512]{2,1,0:T(8,128)(2,1)} %param.10) | copy-start | bytes 1572868
  236.3 1.2 copy-start.1
  237.5 44.4 %copy-start.6 = (f32[512,512]{1,0:T(8,128)}, f32[512,512]{1,0:T(8,128)S(1)}, u32[]{:S(2)}) copy-start(f32[512,512]{1,0:T(8,128)S(1)} %convolution_multiply_fusion) | copy-start | bytes 3145732
  238.2 4.5 collective-permute-start
  285.3 4.5 collective-permute-start.1
  328.6 4.5 collective-permute-start.2
  372.0 4.9 collective-permute-start.3
  415.4 6.0 %collective-permute-start.4 = (f32[512,8]{0,1:T(8,128)S(1)}, f32[512,8]{0,1:T(8,128)S(1)}, u32[]{:S(2)}, u32[]{:S(2)}) collective-permute-start(f32[512,8]{0,1:T(8,128)S(1)} %convolution_add_fusion.3), channel_id=1, source_target_pairs={{64,0},{128,64},{192,128},{256,192},{320,256},{384,320},{448,384},... | collective-permute-start | bytes 49160 | tf_op jit(solution)/shard_map/ppermute | solution.py:10
  460.0 6.0 %collective-permute-start.5 = (f32[512,8]{0,1:T(8,128)S(1)}, f32[512,8]{0,1:T(8,128)S(1)}, u32[]{:S(2)}, u32[]{:S(2)}) collective-permute-start(f32[512,8]{0,1:T(8,128)S(1)} %convolution_add_fusion.2), channel_id=1, source_target_pairs={{64,0},{128,64},{192,128},{256,192},{320,256},{384,320},{448,384},... | collective-permute-start | bytes 49160 | tf_op jit(solution)/shard_map/ppermute | solution.py:10
  504.6 6.0 %collective-permute-start.6 = (f32[512,8]{0,1:T(8,128)S(1)}, f32[512,8]{0,1:T(8,128)S(1)}, u32[]{:S(2)}, u32[]{:S(2)}) collective-permute-start(f32[512,8]{0,1:T(8,128)S(1)} %convolution_add_fusion.1), channel_id=1, source_target_pairs={{64,0},{128,64},{192,128},{256,192},{320,256},{384,320},{448,384},... | collective-permute-start | bytes 49160 | tf_op jit(solution)/shard_map/ppermute | solution.py:10
  548.6 3.7 copy-start.3
Sparse Core Ops, SparseCore 0:
  18.7 204.5 all-reduce.2
